TPU v7x, 512 devices: a whole 4x4x16 slice. The times are simulated.
512 devices in a mesh: dp: 32 (over y, x, core), wide: 16 (over z).
Axes of the slice: x: 4, y: 4, z: 16, core: 2. Of those that a mesh axis runs over, the one named last changes fastest.
Arguments:
- trunk_out: bfloat16 [16384, 1024], P('dp'), may hold values from -6 to 6
- projection: bfloat16 [1024, 4096], P(None, 'wide'), may hold values from -0.1875 to 0.1875
- transform: bfloat16 [4096, 4096], P('wide'), may hold values from -0.125 to 0.125
- block_mask: int32 [32, 32], P('wide'), may hold values from 0 to 1, as said below
- old_index: bfloat16 [16384, 4096], P('dp', 'wide'), may hold values from -6 to 6
- doc_ids: int32 [16384, 4], P('dp'), may hold values from 0 to 16383, as said below
- labels: int32 [16384, 4], P('dp'), may hold values 0 or 1
Outputs:
- new_embed: bfloat16 [16384, 4096], P('dp', 'wide')
- pair_loss: float32 [16384, 4], P('dp')
- trunk_grad: bfloat16 [16384, 4096], P('dp', 'wide')
Inputs may be any that keep to these rules, and one draw needn't show every extreme that they name: `doc_ids`: in each aligned block of 512 rows, no shard id // 512 is named more than 128 times, and one shard is named exactly 128 times. `block_mask`: each block row has 4 to 24 nonzero entries, and some block row has exactly 24.
All inputs are finite; a program needn't handle non-finite values. No bound on the sum of `labels` on one device may be relied on, other than what follows from the above.
Results may differ from a plain program's by a relative error of at most 0.015.
Values may be sent and summed in bfloat16 or wider, within the bound.
No kernel may reach another device: no remote copies, remote signals or barrier semaphores. Data moves between devices by JAX's collectives and lax.ppermute only.
A program may use at most 128 MiB of HBM per device.

v0:
```python
import math
import jax
import jax.numpy as jnp
from jax import lax
from jax.sharding import PartitionSpec as P

E = 4096
K = 4


def local(trunk_out, projection, transform, block_mask, old_index, doc_ids, labels):
    rows = trunk_out.shape[0]
    e_local = transform.shape[0]
    width = transform.shape[1]
    local_blocks, nblocks = block_mask.shape
    side = e_local // local_blocks
    query = jnp.dot(trunk_out, projection, preferred_element_type=jnp.float32).astype(jnp.bfloat16)
    blocks = transform.reshape(local_blocks, side, nblocks, side)
    masked = (blocks * block_mask[:, None, :, None].astype(jnp.bfloat16)).reshape(e_local, width)
    term = jnp.dot(query, masked, preferred_element_type=jnp.float32)
    new = lax.psum_scatter(
        term.astype(jnp.bfloat16), "wide", scatter_dimension=1, tiled=True
    ).astype(jnp.float32)
    flat = doc_ids.reshape(-1)
    whole = lax.all_gather(old_index, "dp", axis=0, tiled=True)
    old_vec = whole[flat].reshape(rows, K, e_local)
    old_wide = old_vec.astype(jnp.float32)
    scale = 1.0 / math.sqrt(E)
    partial_scores = jnp.einsum("re,rke->rk", new, old_wide)
    score = lax.psum(partial_scores, "wide") * scale
    sign = 2.0 * labels.astype(jnp.float32) - 1.0
    pair_loss = jax.nn.softplus(-sign * score)
    dscore = -sign * jax.nn.sigmoid(-sign * score)
    grad_local = (jnp.einsum("rk,rke->re", dscore, old_wide) * scale).astype(jnp.bfloat16)
    grad_full = lax.all_gather(grad_local, "wide", axis=1, tiled=True)
    trunk_grad = lax.dot_general(
        grad_full, masked, (((1,), (1,)), ((), ())), preferred_element_type=jnp.float32
    )
    return (new.astype(jnp.bfloat16), pair_loss, trunk_grad.astype(jnp.bfloat16))


def solution(mesh):
    return jax.shard_map(
        local,
        mesh=mesh,
        in_specs=(
            P("dp", None),
            P(None, "wide"),
            P("wide", None),
            P("wide", None),
            P("dp", "wide"),
            P("dp", None),
            P("dp", None),
        ),
        out_specs=(P("dp", "wide"), P("dp", None), P("dp", "wide")),
        check_vma=False,
    )
```

profile of v0, /device:TPU:2, one launch (start us, length us, event | category | flops | bytes accessed | tf_op | source)
XLA Modules:
  0.0 241.0 jit_solution(8100249756165127333)
XLA Ops:
  8.0 0.0 copy-start
  8.0 0.0 all-gather.3.cloned.1.call-start
  8.1 0.7 all-gather.3.cloned.1.call-update
  8.7 0.0 reduce-scatter.2.cloned.1.call-start
  8.8 0.7 convert_element_type.23
  9.5 0.3 mul.36
  9.8 0.0 copy-done
  9.8 5.8 %convolution_convert_fusion = bf16[512,4096]{1,0:T(8,128)(2,1)} fusion(bf16[512,1024]{1,0:T(8,128)(2,1)S(1)} %copy-done, bf16[1024,256]{1,0:T(8,128)(2,1)} %param.8, bf16[256,4096]{1,0:T(8,128)(2,1)} %param.9, bf16[32,8,32,128]{3,2,1,0:T(8,128)(2,1)S(1)} %bitcast.21), kind=kOutput, calls=%fused_computation.1 | convolution fusion | flops 1345454080 | bytes 9961472 | tf_op jit(solution)/shard_map/dot_general | solution.py:20
  15.7 0.0 copy-start.2
  15.7 0.0 reduce-scatter.2.cloned.1.call-update
  15.7 0.0 all-gather.5.cloned.1.call-start
  15.7 0.6 copy-done.2
  16.4 0.1 copy.10
  16.5 0.2 reshape.45
  16.7 67.9 %all-gather.3.cloned.1.call-done = bf16[16384,256]{1,0:T(8,128)(2,1)} async-done(((bf16[512,256]{1,0:T(8,128)(2,1)}), bf16[16384,256]{1,0:T(8,128)(2,1)}) %all-gather.3.cloned.1.call-update) | async-done | bytes 8388624 | tf_op jit(solution)/shard_map/all_gather | solution.py:25
  84.7 13.0 %gather_fusion = bf16[2048,256]{1,0:T(8,128)(2,1)} fusion(bf16[16384,256]{1,0:T(8,128)(2,1)} %all-gather.3.cloned.1.call-done, s32[2048]{0:T(1024)S(1)} %broadcast_clamp_fusion), kind=kCustom, calls=%fused_computation | custom fusion | bytes 2105344 | tf_op jit(solution)/shard_map/gather | solution.py:26
  97.7 2.1 reshape.46
  99.8 0.0 reduce-scatter.2.cloned.1.call-done
  99.8 0.0 copy-start.1
  99.8 2.0 fusion.1
  101.8 0.1 copy.12
  101.9 31.8 %psum.7 = f32[512,4]{0,1:T(4,128)S(1)} all-reduce(f32[512,4]{0,1:T(4,128)S(1)} %bitcast.23), channel_id=1, replica_groups=mesh['dp'=32,'wide'=16] {'wide'}, use_global_device_ids=true, to_apply=%region_1.0 | all-reduce | flops 2048 | bytes 16384 | tf_op jit(solution)/shard_map/psum | solution.py:30
  133.8 0.0 copy-done.1
  133.8 0.2 copy.13
  134.0 1.9 fusion.4
  135.9 0.7 fusion
  136.7 0.0 all-gather.5.cloned.1.call-update
  136.7 0.6 compare_select_fusion.1
  137.3 91.4 %all-gather.5.cloned.1.call-done = bf16[512,4096]{1,0:T(8,128)(2,1)} async-done(((bf16[512,256]{1,0:T(8,128)(2,1)}), bf16[512,4096]{1,0:T(8,128)(2,1)}) %all-gather.5.cloned.1.call-update) | async-done | bytes 4194320 | tf_op jit(solution)/shard_map/all_gather | solution.py:35
  228.7 4.9 %convolution_convert_fusion.1 = bf16[512,256]{1,0:T(8,128)(2,1)} fusion(bf16[512,4096]{1,0:T(8,128)(2,1)} %all-gather.5.cloned.1.call-done, bf16[256,4096]{1,0:T(8,128)(2,1)} %param.9, bf16[32,8,32,128]{3,2,1,0:T(8,128)(2,1)S(1)} %bitcast.22), kind=kOutput, calls=%fused_computation.3 | convolution fusion | flops 1074921472 | bytes 8650752 | tf_op jit(solution)/shard_map/dot_general | solution.py:36
  (3 shorter events, 0.0 us)
Async XLA Ops:
  8.0 1.8 copy-start
  8.0 76.7 %all-gather.3.cloned.1.call-start = ((), (), s32[]{:S(2)}) async-start(), calls=%async_computation.2 | async-start | bytes 8650752 | tf_op jit(solution)/shard_map/all_gather | solution.py:25
  8.7 91.1 %reduce-scatter.2.cloned.1.call-start = ((), (), s32[]{:S(2)}) async-start(), calls=%async_computation.1 | async-start | bytes 4456448 | tf_op jit(solution)/shard_map/reduce_scatter | solution.py:21
  15.7 0.7 copy-start.2
  15.7 213.0 %all-gather.5.cloned.1.call-start = ((), (), s32[]{:S(2)}) async-start(), calls=%async_computation.3 | async-start | bytes 4456448 | tf_op jit(solution)/shard_map/all_gather | solution.py:35
  99.8 33.9 %copy-start.1 = (s32[512,4]{0,1:T(4,128)S(1)}, s32[512,4]{0,1:T(4,128)}, u32[]{:S(2)}) copy-start(s32[512,4]{0,1:T(4,128)} %param.13) | copy-start | bytes 24580
Sparse Core Ops, SparseCore 0:
  12.0 72.6 all-gather.2
Sparse Core Ops, SparseCore 1:
  15.8 83.9 reduce-scatter.1
  136.8 91.9 all-gather.4
where the time goes:
time: 241 us
  waiting for transfers between devices  160 us (66%)
  blocking collectives  31.8 us (13%)
  local copies, waits for them, and re-layouts  16.8 us (7%)
  between operations  15.6 us (6%)
  matrix products  14.6 us (6%)
    all_gather x1, waiting for transfers between devices, local(): grad_full = lax.all_gather(grad_local, 'wide', axis=1, tiled=True)  91.4 us
    all_gather x1, waiting for transfers between devices, local(): whole = lax.all_gather(old_index, 'dp', axis=0, tiled=True)  67.9 us
    psum x1, blocking collectives, local(): score = lax.psum(partial_scores, 'wide') * scale  31.8 us
    gather x1, local copies, waits for them, and re-layouts, local(): old_vec = whole[flat].reshape(rows, K, e_local)  13 us
    dot_general x1, matrix products, local(): term = jnp.dot(query, masked, preferred_element_type=jnp.float32)  5.83 us
    dot_general x1, matrix products, local(): lax.dot_general(grad_full, masked, (((1,), (1,)), ((), ())), preferred_el...  4.9 us
  transfers between devices with their start and end apart: 3, of which 2 were waited for; matrix products, arithmetic and copies ran while one was open for 10% of the time, Pallas kernels for 0%

commit v1 on v0

--- a/solution.py
+++ b/solution.py
@@ -32,7 +32,9 @@
     pair_loss = jax.nn.softplus(-sign * score)
     dscore = -sign * jax.nn.sigmoid(-sign * score)
     grad_local = (jnp.einsum("rk,rke->re", dscore, old_wide) * scale).astype(jnp.bfloat16)
-    grad_full = lax.all_gather(grad_local, "wide", axis=1, tiled=True)
+    grad_full = jnp.concatenate(
+        lax.all_to_all(jnp.stack([grad_local] * lax.axis_size("wide")), "wide", 0, 0), axis=1
+    )
     trunk_grad = lax.dot_general(
         grad_full, masked, (((1,), (1,)), ((), ())), preferred_element_type=jnp.float32
     )

time: 241 us -> 341 us (1.41)
  the two profiles are of different devices: /device:TPU:2 before, /device:TPU:32 now
where the time goes in v1:
time: 341 us
  blocking collectives  220 us (65%)
  waiting for transfers between devices  68.3 us (20%)
  local copies, waits for them, and re-layouts  19.2 us (6%)
  between operations  15.6 us (5%)
  matrix products  10.4 us (3%)
  other arithmetic  7.1 us (2%)
    all_to_all x1, blocking collectives, local(): lax.all_to_all(jnp.stack([grad_local] * lax.axis_size('wide')), 'wide', 0...  190 us
    all_gather x1, waiting for transfers between devices, local(): whole = lax.all_gather(old_index, 'dp', axis=0, tiled=True)  67.6 us
    psum x1, blocking collectives, local(): score = lax.psum(partial_scores, 'wide') * scale  30.4 us
    gather x1, local copies, waits for them, and re-layouts, local(): old_vec = whole[flat].reshape(rows, K, e_local)  13 us
  transfers between devices with their start and end apart: 2, of which 1 were waited for; matrix products, arithmetic and copies ran while one was open for 7% of the time, Pallas kernels for 0%

profile of v1, /device:TPU:32, one launch (start us, length us, event | category | flops | bytes accessed | tf_op | source)
XLA Modules:
  0.0 340.9 jit_solution(11397983756455690459)
XLA Ops:
  8.0 0.0 copy-start
  8.0 0.0 all-gather.2.cloned.1.call-start
  8.1 0.7 all-gather.2.cloned.1.call-update
  8.7 0.0 reduce-scatter.2.cloned.1.call-start
  8.8 0.7 convert_element_type.23
  9.5 0.3 mul.36
  9.8 0.0 copy-done
  9.8 5.8 %convolution_convert_fusion = bf16[512,4096]{1,0:T(8,128)(2,1)} fusion(bf16[512,1024]{1,0:T(8,128)(2,1)S(1)} %copy-done, bf16[1024,256]{1,0:T(8,128)(2,1)} %param.8, bf16[256,4096]{1,0:T(8,128)(2,1)} %param.9, bf16[32,8,32,128]{3,2,1,0:T(8,128)(2,1)S(1)} %bitcast.16), kind=kOutput, calls=%fused_computation.1 | convolution fusion | flops 1345454080 | bytes 9961472 | tf_op jit(solution)/shard_map/dot_general | solution.py:20
  15.7 0.0 copy-start.2
  15.7 0.0 reduce-scatter.2.cloned.1.call-update
  15.7 0.7 copy-done.2
  16.3 0.1 copy.10
  16.5 0.2 reshape.53
  16.7 67.6 %all-gather.2.cloned.1.call-done = bf16[16384,256]{1,0:T(8,128)(2,1)} async-done(((bf16[512,256]{1,0:T(8,128)(2,1)}), bf16[16384,256]{1,0:T(8,128)(2,1)}) %all-gather.2.cloned.1.call-update) | async-done | bytes 8388624 | tf_op jit(solution)/shard_map/all_gather | solution.py:25
  84.3 13.0 %gather_fusion = bf16[2048,256]{1,0:T(8,128)(2,1)} fusion(bf16[16384,256]{1,0:T(8,128)(2,1)} %all-gather.2.cloned.1.call-done, s32[2048]{0:T(1024)S(1)} %broadcast_clamp_fusion), kind=kCustom, calls=%fused_computation | custom fusion | bytes 2105344 | tf_op jit(solution)/shard_map/gather | solution.py:26
  97.4 2.1 reshape.54
  99.5 0.0 reduce-scatter.2.cloned.1.call-done
  99.5 0.0 copy-start.3
  99.5 2.0 fusion
  101.5 0.1 copy.12
  101.6 30.4 %psum.7 = f32[512,4]{0,1:T(4,128)S(1)} all-reduce(f32[512,4]{0,1:T(4,128)S(1)} %bitcast.19), channel_id=1, replica_groups=mesh['dp'=32,'wide'=16] {'wide'}, use_global_device_ids=true, to_apply=%region_1.0 | all-reduce | flops 2048 | bytes 16384 | tf_op jit(solution)/shard_map/psum | solution.py:30
  132.0 0.0 copy-done.3
  132.0 0.6 divide_multiply_fusion
  132.7 0.1 copy.17
  132.8 4.7 %multiply_reduce_fusion = f32[512,256]{1,0:T(8,128)} fusion(bf16[512,4,256]{2,1,0:T(4,128)(2,1)} %reshape.54, f32[512,4]{1,0:T(8,128)S(1)} %copy.17), kind=kLoop, calls=%fused_computation.3 | loop fusion | flops 1441792 | bytes 1581056
  137.5 2.0 copy.16
  139.5 1.1 multiply_convert_fusion
  140.6 0.4 stack.2
  141.0 0.0 copy-start.1
  141.0 189.9 %all_to_all.5 = bf16[16,512,256]{1,2,0:T(8,128)(2,1)S(1)} all-to-all(bf16[16,512,256]{1,2,0:T(8,128)(2,1)S(1)} %stack.2), channel_id=1, replica_groups=mesh['dp'=32,'wide'=16] {'wide'}, dimensions={0} | all-to-all | bytes 8388608 | tf_op jit(solution)/shard_map/all_to_all | solution.py:36
  330.9 0.0 copy-done.1
  330.9 2.6 convolution_convert_fusion.1
  (2 shorter events, 0.0 us)
Async XLA Ops:
  8.0 1.8 copy-start
  8.0 76.3 %all-gather.2.cloned.1.call-start = ((), (), s32[]{:S(2)}) async-start(), calls=%async_computation.3 | async-start | bytes 8650752 | tf_op jit(solution)/shard_map/all_gather | solution.py:25
  8.7 90.8 %reduce-scatter.2.cloned.1.call-start = ((), (), s32[]{:S(2)}) async-start(), calls=%async_computation.2 | async-start | bytes 4456448 | tf_op jit(solution)/shard_map/reduce_scatter | solution.py:21
  15.7 0.7 copy-start.2
  99.5 32.5 %copy-start.3 = (s32[512,4]{0,1:T(4,128)S(1)}, s32[512,4]{0,1:T(4,128)}, u32[]{:S(2)}) copy-start(s32[512,4]{0,1:T(4,128)} %param.13) | copy-start | bytes 24580
  141.0 189.9 %copy-start.1 = (bf16[256,4096]{1,0:T(8,128)(2,1)S(1)}, bf16[256,4096]{1,0:T(8,128)(2,1)}, u32[]{:S(2)}) copy-start(bf16[256,4096]{1,0:T(8,128)(2,1)} %param.9) | copy-start | bytes 6291460
Sparse Core Ops, SparseCore 0:
  12.0 72.2 all-gather.1
Sparse Core Ops, SparseCore 1:
  15.8 83.3 reduce-scatter.1

commit v2 on v0

--- a/solution.py
+++ b/solution.py
@@ -22,7 +22,11 @@
         term.astype(jnp.bfloat16), "wide", scatter_dimension=1, tiled=True
     ).astype(jnp.float32)
     flat = doc_ids.reshape(-1)
-    whole = lax.all_gather(old_index, "dp", axis=0, tiled=True)
+    size = lax.axis_size("dp")
+    repeats = [size if d == 0 else 1 for d in range(old_index.ndim)]
+    whole = lax.all_to_all(
+        jnp.tile(old_index, repeats), "dp", split_axis=0, concat_axis=0, tiled=True
+    )
     old_vec = whole[flat].reshape(rows, K, e_local)
     old_wide = old_vec.astype(jnp.float32)
     scale = 1.0 / math.sqrt(E)

time: 241 us -> 289 us (1.20)
  waiting for transfers between devices: 160 us -> 192 us
  starting transfers between devices: 0.13 us -> 10.7 us
  local copies, waits for them, and re-layouts: 16.8 us -> 21.2 us
    all_to_all x0 -> x1, waiting for transfers between devices: none -> 99.3 us  [local(): lax.all_to_all(jnp.tile(old_index, repeats), 'dp', split_axis=0, concat_a...]
    all_gather x1 -> x0, waiting for transfers between devices: 67.9 us -> none  [local(): whole = lax.all_gather(old_index, 'dp', axis=0, tiled=True)]
    all_to_all x0 -> x1, starting transfers between devices: none -> 10.6 us  [local(): lax.all_to_all(jnp.tile(old_index, repeats), 'dp', split_axis=0, concat_a...]
    another operation x0 -> x1, local copies, waits for them, and re-layouts: none -> 4.17 us  [local(): jnp.tile(old_index, repeats)]
  transfers between devices with their start and end apart: 3 -> 3, of which waited for: 2 -> 2; matrix products, arithmetic and copies ran while one was open for 10% -> 7% of each run, Pallas kernels for 0% -> 0%
where the time goes in v2:
time: 289 us
  waiting for transfers between devices  192 us (66%)
  blocking collectives  34.1 us (12%)
  local copies, waits for them, and re-layouts  21.2 us (7%)
  matrix products  14.6 us (5%)
  between operations  14.1 us (5%)
  starting transfers between devices  10.7 us (4%)
    all_to_all x1, waiting for transfers between devices, local(): lax.all_to_all(jnp.tile(old_index, repeats), 'dp', split_axis=0, concat_a...  99.3 us
    all_gather x1, waiting for transfers between devices, local(): grad_full = lax.all_gather(grad_local, 'wide', axis=1, tiled=True)  92.6 us
    psum x1, blocking collectives, local(): score = lax.psum(partial_scores, 'wide') * scale  34.1 us
    gather x1, local copies, waits for them, and re-layouts, local(): old_vec = whole[flat].reshape(rows, K, e_local)  12.9 us
    all_to_all x1, starting transfers between devices, local(): lax.all_to_all(jnp.tile(old_index, repeats), 'dp', split_axis=0, concat_a...  10.6 us
    dot_general x1, matrix products, local(): term = jnp.dot(query, masked, preferred_element_type=jnp.float32)  5.79 us
  transfers between devices with their start and end apart: 3, of which 2 were waited for; matrix products, arithmetic and copies ran while one was open for 7% of the time, Pallas kernels for 0%

profile of v2, /device:TPU:2, one launch (start us, length us, event | category | flops | bytes accessed | tf_op | source)
XLA Modules:
  0.0 288.9 jit_solution(991492953106576501)
XLA Ops:
  7.2 0.0 copy-start
  7.2 0.0 reduce-scatter.2.cloned.1.call-start
  7.2 0.8 convert_element_type.23
  8.0 0.3 mul.36
  8.3 0.1 copy-done
  8.4 5.8 %convolution_convert_fusion = bf16[512,4096]{1,0:T(8,128)(2,1)} fusion(bf16[512,1024]{1,0:T(8,128)(2,1)S(1)} %copy-done, bf16[1024,256]{1,0:T(8,128)(2,1)} %param.8, bf16[256,4096]{1,0:T(8,128)(2,1)} %param.9, bf16[32,8,32,128]{3,2,1,0:T(8,128)(2,1)S(1)} %bitcast.22), kind=kOutput, calls=%fused_computation.1 | convolution fusion | flops 1345454080 | bytes 9961472 | tf_op jit(solution)/shard_map/dot_general | solution.py:20
  14.2 0.0 copy-start.1
  14.2 0.0 reduce-scatter.2.cloned.1.call-update
  14.2 0.9 copy-done.1
  15.2 4.2 %tile.2 = bf16[32,512,256]{2,1,0:T(8,128)(2,1)} broadcast(bf16[512,256]{1,0:T(8,128)(2,1)S(1)} %copy-done.1), dimensions={1,2} | broadcast | bytes 8650752 | tf_op jit(solution)/shard_map/tile | solution.py:28
  19.3 0.0 copy-start.3
  19.3 10.6 %all-to-all-start = ((bf16[32,512,256]{2,1,0:T(8,128)(2,1)}), bf16[32,512,256]{2,1,0:T(8,128)(2,1)}, u32[]{:S(2)}, u32[]{:S(2)}) async-start(bf16[32,512,256]{2,1,0:T(8,128)(2,1)} %tile.2), calls=%async_computation.1 | async-start | bytes 16777216 | tf_op jit(solution)/shard_map/all_to_all | solution.py:27
  29.9 0.0 all-gather.2.cloned.1.call-start
  30.0 0.0 copy-done.3
  30.0 0.1 copy.10
  30.1 0.2 reshape.52
  30.4 99.3 %all-to-all-done = bf16[32,512,256]{2,1,0:T(8,128)(2,1)} async-done(((bf16[32,512,256]{2,1,0:T(8,128)(2,1)}), bf16[32,512,256]{2,1,0:T(8,128)(2,1)}, u32[]{:S(2)}, u32[]{:S(2)}) %all-to-all-start) | async-done | bytes 8388640 | tf_op jit(solution)/shard_map/all_to_all | solution.py:27
  129.7 12.9 %gather_fusion = bf16[2048,256]{1,0:T(8,128)(2,1)} fusion(bf16[16384,256]{1,0:T(8,128)(2,1)} %bitcast.1, s32[2048]{0:T(1024)S(1)} %broadcast_clamp_fusion), kind=kCustom, calls=%fused_computation | custom fusion | bytes 2105344 | tf_op jit(solution)/shard_map/gather | solution.py:30
  142.6 2.1 reshape.53
  144.7 0.0 reduce-scatter.2.cloned.1.call-done
  144.7 0.0 copy-start.2
  144.7 2.0 fusion.1
  146.7 0.1 copy.12
  146.9 34.1 %psum.7 = f32[512,4]{0,1:T(4,128)S(1)} all-reduce(f32[512,4]{0,1:T(4,128)S(1)} %bitcast.24), channel_id=1, replica_groups=mesh['dp'=32,'wide'=16] {'wide'}, use_global_device_ids=true, to_apply=%region_1.0 | all-reduce | flops 2048 | bytes 16384 | tf_op jit(solution)/shard_map/psum | solution.py:34
  181.0 0.0 copy-done.2
  181.1 0.2 copy.13
  181.3 1.9 fusion.4
  183.2 0.7 fusion
  183.9 0.0 all-gather.2.cloned.1.call-update
  183.9 0.6 compare_select_fusion.1
  184.6 92.6 %all-gather.2.cloned.1.call-done = bf16[512,4096]{1,0:T(8,128)(2,1)} async-done(((bf16[512,256]{1,0:T(8,128)(2,1)}), bf16[512,4096]{1,0:T(8,128)(2,1)}) %all-gather.2.cloned.1.call-update) | async-done | bytes 4194320 | tf_op jit(solution)/shard_map/all_gather | solution.py:39
  277.2 4.9 %convolution_convert_fusion.1 = bf16[512,256]{1,0:T(8,128)(2,1)} fusion(bf16[512,4096]{1,0:T(8,128)(2,1)} %all-gather.2.cloned.1.call-done, bf16[256,4096]{1,0:T(8,128)(2,1)} %param.9, bf16[32,8,32,128]{3,2,1,0:T(8,128)(2,1)S(1)} %bitcast.23), kind=kOutput, calls=%fused_computation.3 | convolution fusion | flops 1074921472 | bytes 8650752 | tf_op jit(solution)/shard_map/dot_general | solution.py:40
  (3 shorter events, 0.0 us)
Async XLA Ops:
  7.2 1.2 copy-start
  7.2 137.6 %reduce-scatter.2.cloned.1.call-start = ((), (), s32[]{:S(2)}) async-start(), calls=%async_computation.2 | async-start | bytes 4456448 | tf_op jit(solution)/shard_map/reduce_scatter | solution.py:21
  14.2 0.9 copy-start.1
  19.3 10.7 %copy-start.3 = (s32[512,4]{0,1:T(4,128)S(1)}, s32[512,4]{0,1:T(4,128)}, u32[]{:S(2)}) copy-start(s32[512,4]{0,1:T(4,128)} %param.12) | copy-start | bytes 24580
  19.3 110.3 %all-to-all-start = ((bf16[32,512,256]{2,1,0:T(8,128)(2,1)}), bf16[32,512,256]{2,1,0:T(8,128)(2,1)}, u32[]{:S(2)}, u32[]{:S(2)}) async-start(bf16[32,512,256]{2,1,0:T(8,128)(2,1)} %tile.2), calls=%async_computation.1 | async-start | bytes 16777216 | tf_op jit(solution)/shard_map/all_to_all | solution.py:27
  29.9 247.2 %all-gather.2.cloned.1.call-start = ((), (), s32[]{:S(2)}) async-start(), calls=%async_computation.3 | async-start | bytes 4456448 | tf_op jit(solution)/shard_map/all_gather | solution.py:39
  144.7 36.3 %copy-start.2 = (s32[512,4]{0,1:T(4,128)S(1)}, s32[512,4]{0,1:T(4,128)}, u32[]{:S(2)}) copy-start(s32[512,4]{0,1:T(4,128)} %param.13) | copy-start | bytes 24580
Sparse Core Ops, SparseCore 0:
  14.4 83.5 reduce-scatter.1
  184.1 93.0 all-gather.1
